TPU v7x, 256 devices: a whole 4x4x8 slice. The times are simulated.
256 devices in a mesh: blocks: 64 (over z, x, core), chan: 4 (over y).
Axes of the slice: x: 4, y: 4, z: 8, core: 2. Of those that a mesh axis runs over, the one named last changes fastest.
Arguments:
- fine_input: bfloat16 [1024, 64, 512], P('blocks', 'chan'), may hold values from -6 to 6
- block_counts: int32 [64], replicated, may hold values from 8 to 16, as said below
- fine_weight: bfloat16 [7, 64, 64], P(None, 'chan'), may hold values from -0.25 to 0.25
- fine_bias: float32 [64], P('chan'), may hold values from -3 to 3
- coarse_weight: bfloat16 [7, 64, 64], P(None, 'chan'), may hold values from -0.25 to 0.25
- coarse_bias: float32 [64], P('chan'), may hold values from -3 to 3
- coarse_cotangent: bfloat16 [128, 64, 512], P('blocks', 'chan'), may hold values from -48 to 48
Outputs:
- coarser_level_output: bfloat16 [128, 64, 512], P('blocks', 'chan')
- fine_grad: bfloat16 [1024, 64, 512], P('blocks', 'chan')
- fine_weight_grad: float32 [7, 64, 64], P(None, 'chan')
- fine_bias_grad: float32 [64], P('chan')
- coarse_weight_grad: float32 [7, 64, 64], P(None, 'chan')
- coarse_bias_grad: float32 [64], P('chan')
Inputs may be any that keep to these rules, and one draw needn't show every extreme that they name: `block_counts`: fine blocks held by each device of blocks; they sum to 768, and some device holds exactly 16.
All inputs are finite; a program needn't handle non-finite values.
Results may differ from a plain program's by a relative error of at most 0.017.
Values may be sent and summed in bfloat16 or wider, within the bound.
No kernel may reach another device: no remote copies, remote signals or barrier semaphores. Data moves between devices by JAX's collectives and lax.ppermute only.
A program may use at most 64 MiB of HBM per device.

v0:
```python
import jax
import jax.numpy as jnp
from jax import lax
from jax.sharding import PartitionSpec as P

EDGE = 8
TAP_PAIRS = (0, 2, 1, 4, 3, 6, 5)


def from_behind(block, axis, distance):
    devices = range(lax.axis_size(axis))
    route = [(i - distance, i) for i in devices if i - distance in devices]
    return lax.ppermute(block, axis, route)


def block_layers(block_cube):
    channels, edge_cells = (block_cube.shape[0], block_cube.shape[1])
    side_layers = [
        block_cube[:, :, :, 0],
        block_cube[:, :, :, -1],
        block_cube[:, :, 0, :],
        block_cube[:, :, -1, :],
        block_cube[:, 0],
        block_cube[:, -1],
    ]
    return jnp.stack(side_layers).reshape(6, channels, edge_cells * edge_cells)


def block_views(block_cube, halo_layers):
    channels, edge_cells = (block_cube.shape[0], block_cube.shape[1])
    sheets = halo_layers.reshape(6, channels, edge_cells, edge_cells)
    minus_x = jnp.concatenate([sheets[0][:, :, :, None], block_cube[:, :, :, :-1]], axis=3)
    plus_x = jnp.concatenate([block_cube[:, :, :, 1:], sheets[1][:, :, :, None]], axis=3)
    minus_y = jnp.concatenate([sheets[2][:, :, None, :], block_cube[:, :, :-1, :]], axis=2)
    plus_y = jnp.concatenate([block_cube[:, :, 1:, :], sheets[3][:, :, None, :]], axis=2)
    minus_z = jnp.concatenate([sheets[4][:, None], block_cube[:, :-1]], axis=1)
    plus_z = jnp.concatenate([block_cube[:, 1:], sheets[5][:, None]], axis=1)
    stacked = jnp.stack([block_cube, minus_x, plus_x, minus_y, plus_y, minus_z, plus_z])
    return stacked.reshape(7 * channels, edge_cells**3)


def slope_of(pre_values):
    sigmoid_values = jax.nn.sigmoid(pre_values)
    return sigmoid_values * (1.0 + pre_values * (1.0 - sigmoid_values))


def fine_halo(layer_table, block_ids, first_block, live_count, total_blocks):
    slot_count = layer_table.shape[0]
    plus_side = layer_table[:, 1::2]
    minus_side = layer_table[:, 0::2]
    tail_layers = lax.dynamic_slice_in_dim(plus_side, live_count - 4, 4, 0)
    from_lower = from_behind(tail_layers, "blocks", 1)
    from_upper = from_behind(minus_side[:4], "blocks", -1)
    table_minus = jnp.concatenate([from_lower, plus_side], axis=0)
    table_plus = jnp.concatenate([minus_side, from_upper], axis=0)
    strides = jnp.array([1, 2, 4], jnp.int32)
    lower_ids = block_ids[:, None] - strides[None, :]
    upper_octant_index = block_ids[:, None] + strides[None, :]
    end_block = first_block + live_count
    rows_minus = jnp.clip(lower_ids - first_block + 4, 0, slot_count + 3)
    rows_plus = jnp.clip(
        jnp.where(
            upper_octant_index < end_block,
            upper_octant_index - first_block,
            slot_count + upper_octant_index - end_block,
        ),
        0,
        slot_count + 3,
    )
    columns = jnp.arange(3, dtype=jnp.int32)[None, :]
    got_minus = table_minus[rows_minus, columns]
    got_plus = table_plus[rows_plus, columns]
    parity_x = block_ids % 2
    parity_y = block_ids // 2 % 2
    keep_minus = jnp.stack([parity_x == 1, parity_y == 1, block_ids >= 4], axis=1)
    keep_plus = jnp.stack([parity_x == 0, parity_y == 0, block_ids + 4 < total_blocks], axis=1)
    zero_value = jnp.zeros((), layer_table.dtype)
    got_minus = jnp.where(keep_minus[:, :, None, None], got_minus, zero_value)
    got_plus = jnp.where(keep_plus[:, :, None, None], got_plus, zero_value)
    merged = jnp.stack([got_minus, got_plus], axis=2)
    return merged.reshape(layer_table.shape)


def coarse_halo(layer_table, coarse_ids, coarse_first, coarse_count, coarse_total):
    slot_count = layer_table.shape[0]
    top_layers = layer_table[:, 5]
    bottom_layers = layer_table[:, 4]
    last_top = lax.dynamic_index_in_dim(top_layers, coarse_count - 1, 0, keepdims=False)
    from_lower = from_behind(last_top, "blocks", 1)
    from_upper = from_behind(bottom_layers[0], "blocks", -1)
    table_minus = jnp.concatenate([from_lower[None], top_layers], axis=0)
    table_plus = jnp.concatenate([bottom_layers, from_upper[None]], axis=0)
    rows_minus = jnp.clip(coarse_ids - coarse_first, 0, slot_count)
    rows_plus = jnp.clip(
        jnp.where(
            coarse_ids + 1 < coarse_first + coarse_count, coarse_ids + 1 - coarse_first, slot_count
        ),
        0,
        slot_count,
    )
    zero_value = jnp.zeros((), layer_table.dtype)
    below_layer = jnp.where((coarse_ids >= 1)[:, None, None], table_minus[rows_minus], zero_value)
    above_layer = jnp.where(
        (coarse_ids + 1 < coarse_total)[:, None, None], table_plus[rows_plus], zero_value
    )
    flat_zero = jnp.zeros_like(below_layer)
    return jnp.stack([flat_zero, flat_zero, flat_zero, flat_zero, below_layer, above_layer], axis=1)


def apply_blocks(matrix, block_cubes, halo_table):

    def one_block(operands):
        return jnp.dot(
            matrix, block_views(operands[0], operands[1]), preferred_element_type=jnp.float32
        )

    return lax.map(one_block, (block_cubes, halo_table))


def weight_block(operands):
    tap_views = block_views(operands[0], operands[1])
    return lax.dot_general(
        operands[2], tap_views, (((1,), (1,)), ((), ())), preferred_element_type=jnp.float32
    )


def restrict_blocks(hidden, half_edge):
    count, width = (hidden.shape[0], hidden.shape[1])
    shaped = hidden.reshape(count, width, half_edge, 2, half_edge, 2, half_edge, 2)
    return (
        (jnp.sum(shaped, axis=(3, 5, 7), dtype=jnp.float32) * 0.125)
        .astype(jnp.bfloat16)
        .reshape(count, width, half_edge**3)
    )


def sum_over_blocks(parts):
    chan_index = lax.axis_index("chan")
    chan_count = lax.axis_size("chan")
    flat = jnp.concatenate([part.reshape(-1) for part in parts])
    slots = jnp.zeros((chan_count, flat.shape[0]), flat.dtype)
    slots = lax.dynamic_update_index_in_dim(slots, flat, chan_index, 0)
    summed = lax.psum(slots, ("blocks", "chan"))
    mine = lax.dynamic_index_in_dim(summed, chan_index, 0, keepdims=False)
    pieces = []
    offset = 0
    for part in parts:
        pieces.append(mine[offset : offset + part.size].reshape(part.shape))
        offset += part.size
    return tuple(pieces)


def local(
    fine_input, block_counts, fine_weight, fine_bias, coarse_weight, coarse_bias, coarse_cotangent
):
    slot_count, group_size, cell_count = fine_input.shape
    coarse_slots = coarse_cotangent.shape[0]
    channels = fine_weight.shape[2]
    half_edge = EDGE // 2
    octant_cells = half_edge**3
    pair_index = jnp.array(TAP_PAIRS, jnp.int32)
    device = lax.axis_index("blocks")
    starts = jnp.cumsum(block_counts) - block_counts
    first_block = starts[device]
    live_count = block_counts[device]
    end_block = first_block + live_count
    total_blocks = jnp.sum(block_counts)
    coarse_total = total_blocks // 8
    coarse_first = (first_block + 7) // 8
    coarse_count = (end_block + 7) // 8 - coarse_first
    block_ids = first_block + jnp.arange(slot_count, dtype=jnp.int32)
    coarse_ids = coarse_first + jnp.arange(coarse_slots, dtype=jnp.int32)
    live_mask = (jnp.arange(slot_count) < live_count)[:, None, None]
    coarse_live = (jnp.arange(coarse_slots) < coarse_count)[:, None, None]
    full_input = lax.all_gather(fine_input, "chan", axis=1, tiled=True)
    fine_cubes = full_input.reshape(slot_count, channels, EDGE, EDGE, EDGE)
    input_halos = fine_halo(
        jax.vmap(block_layers)(fine_cubes), block_ids, first_block, live_count, total_blocks
    )
    forward_fine = fine_weight.transpose(1, 0, 2).reshape(group_size, 7 * channels)
    fine_views = jax.vmap(block_views)(fine_cubes, input_halos)
    pre_fine = (
        jnp.einsum("ln,bnp->blp", forward_fine, fine_views, preferred_element_type=jnp.float32)
        + fine_bias[None, :, None]
    )
    octants = restrict_blocks(jax.nn.silu(pre_fine).astype(jnp.bfloat16), half_edge)
    upper_octants = from_behind(octants[:7], "blocks", -1)
    octant_table = jnp.concatenate([octants, upper_octants], axis=0)
    children = coarse_ids[:, None] * 8 + jnp.arange(8, dtype=jnp.int32)[None, :]
    child_rows = jnp.clip(
        jnp.where(children < end_block, children - first_block, slot_count + children - end_block),
        0,
        slot_count + 6,
    )
    gathered = octant_table[child_rows]
    coarse_local = (
        gathered.reshape(coarse_slots, 2, 2, 2, group_size, half_edge, half_edge, half_edge)
        .transpose(0, 4, 1, 5, 2, 6, 3, 7)
        .reshape(coarse_slots, group_size, cell_count)
    )
    coarse_local = jnp.where(coarse_live, coarse_local, jnp.zeros((), jnp.bfloat16))
    coarse_full = lax.all_gather(coarse_local, "chan", axis=1, tiled=True)
    coarse_cubes = coarse_full.reshape(coarse_slots, channels, EDGE, EDGE, EDGE)
    coarse_in_halos = coarse_halo(
        jax.vmap(block_layers)(coarse_cubes), coarse_ids, coarse_first, coarse_count, coarse_total
    )
    coarser_level_views = jax.vmap(block_views)(coarse_cubes, coarse_in_halos)
    forward_coarser_level = coarse_weight.transpose(1, 0, 2).reshape(group_size, 7 * channels)
    pre_coarse = (
        jnp.einsum(
            "ln,enp->elp",
            forward_coarser_level,
            coarser_level_views,
            preferred_element_type=jnp.float32,
        )
        + coarse_bias[None, :, None]
    )
    coarser_level_output = jnp.where(coarse_live, jax.nn.silu(pre_coarse), 0.0).astype(jnp.bfloat16)
    coarser_level_delta = jnp.where(
        coarse_live, coarse_cotangent.astype(jnp.float32) * slope_of(pre_coarse), 0.0
    ).astype(jnp.bfloat16)
    coarse_weight_grad = jnp.einsum(
        "zlc,znc->ln", coarser_level_delta, coarser_level_views, preferred_element_type=jnp.float32
    )
    coarse_weight_grad = coarse_weight_grad.reshape(group_size, 7, channels).transpose(1, 0, 2)
    coarse_bias_grad = jnp.sum(coarser_level_delta, axis=(0, 2), dtype=jnp.float32)
    delta_cubes = coarser_level_delta.reshape(coarse_slots, group_size, EDGE, EDGE, EDGE)
    delta_halos = coarse_halo(
        jax.vmap(block_layers)(delta_cubes), coarse_ids, coarse_first, coarse_count, coarse_total
    )
    delta_window_views = jax.vmap(block_views)(delta_cubes, delta_halos)
    backward_coarser_level = (
        coarse_weight[pair_index].transpose(2, 0, 1).reshape(channels, 7 * group_size)
    )
    partial_sums = jnp.einsum(
        "ur,mre->mue",
        backward_coarser_level,
        delta_window_views,
        preferred_element_type=jnp.float32,
    )
    coarse_back = lax.psum_scatter(
        partial_sums.astype(jnp.bfloat16), "chan", scatter_dimension=1, tiled=True
    ).astype(jnp.float32)
    coarse_back = jnp.where(coarse_live, coarse_back, 0.0).astype(jnp.bfloat16)
    coarse_octants = (
        coarse_back.reshape(coarse_slots, group_size, 2, half_edge, 2, half_edge, 2, half_edge)
        .transpose(0, 2, 4, 6, 1, 3, 5, 7)
        .reshape(coarse_slots * 8, group_size, octant_cells)
    )
    last_octants = lax.dynamic_slice_in_dim(coarse_octants, (coarse_count - 1) * 8 + 1, 7, 0)
    lower_octants = from_behind(last_octants, "blocks", 1)
    back_table = jnp.concatenate([coarse_octants, lower_octants], axis=0)
    parents = block_ids // 8
    octant_ids = block_ids % 8
    back_rows = jnp.clip(
        jnp.where(
            parents >= coarse_first,
            (parents - coarse_first) * 8 + octant_ids,
            coarse_slots * 8 + octant_ids - 1,
        ),
        0,
        coarse_slots * 8 + 6,
    )
    picked_rows = back_table[back_rows]
    picked = picked_rows.reshape(slot_count, group_size, half_edge, 1, half_edge, 1, half_edge, 1)
    widened = jnp.broadcast_to(
        picked, (slot_count, group_size, half_edge, 2, half_edge, 2, half_edge, 2)
    ).reshape(slot_count, group_size, cell_count)
    fine_delta = jnp.where(
        live_mask, widened.astype(jnp.float32) * 0.125 * slope_of(pre_fine), 0.0
    ).astype(jnp.bfloat16)
    fine_weight_grad = jnp.einsum(
        "blp,bnp->ln", fine_delta, fine_views, preferred_element_type=jnp.float32
    )
    fine_weight_grad = fine_weight_grad.reshape(group_size, 7, channels).transpose(1, 0, 2)
    fine_bias_grad = jnp.sum(fine_delta, axis=(0, 2), dtype=jnp.float32)
    fine_delta_cubes = fine_delta.reshape(slot_count, group_size, EDGE, EDGE, EDGE)
    fine_delta_halos = fine_halo(
        jax.vmap(block_layers)(fine_delta_cubes), block_ids, first_block, live_count, total_blocks
    )
    back_fine = fine_weight[pair_index].transpose(2, 0, 1).reshape(channels, 7 * group_size)
    fine_delta_views = jax.vmap(block_views)(fine_delta_cubes, fine_delta_halos)
    fine_partial = jnp.einsum(
        "ur,bre->bue", back_fine, fine_delta_views, preferred_element_type=jnp.float32
    )
    fine_back = lax.psum_scatter(
        fine_partial.astype(jnp.bfloat16), "chan", scatter_dimension=1, tiled=True
    ).astype(jnp.float32)
    fine_grad = jnp.where(live_mask, fine_back, 0.0).astype(jnp.bfloat16)
    fine_weight_grad, fine_bias_grad, coarse_weight_grad, coarse_bias_grad = sum_over_blocks(
        (fine_weight_grad, fine_bias_grad, coarse_weight_grad, coarse_bias_grad)
    )
    fine_norm = jnp.sqrt(total_blocks.astype(jnp.float32) * cell_count)
    coarse_norm = jnp.sqrt(coarse_total.astype(jnp.float32) * cell_count)
    return (
        coarser_level_output,
        fine_grad,
        fine_weight_grad / fine_norm,
        fine_bias_grad / fine_norm,
        coarse_weight_grad / coarse_norm,
        coarse_bias_grad / coarse_norm,
    )


def solution(mesh):
    placed = (
        P("blocks", "chan", None),
        P(),
        P(None, "chan", None),
        P("chan"),
        P(None, "chan", None),
        P("chan"),
        P("blocks", "chan", None),
    )
    return jax.shard_map(
        local,
        mesh=mesh,
        in_specs=placed,
        out_specs=(
            P("blocks", "chan", None),
            P("blocks", "chan", None),
            P(None, "chan", None),
            P("chan"),
            P(None, "chan", None),
            P("chan"),
        ),
        check_vma=False,
    )
```

profile of v0, /device:TPU:6, one launch (start us, length us, event | category | flops | bytes accessed | tf_op | source)
XLA Modules:
  0.0 571.9 jit_solution(10096941222904606873)
XLA Ops:
  26.3 13.6 %all-gather.2.cloned.1.call-done = bf16[16,64,512]{2,0,1:T(8,128)(2,1)} async-done(((bf16[16,16,512]{2,0,1:T(8,128)(2,1)}), bf16[16,64,512]{2,0,1:T(8,128)(2,1)}) %all-gather.2.cloned.1.call-update) | async-done | bytes 1048592 | tf_op jit(solution)/shard_map/all_gather | solution.py:175
  43.4 2.9 fusion.73
  49.3 3.0 fusion.71
  54.9 3.6 collective-permute-start.1
  85.4 33.5 %copy.344 = bf16[16,7,64,8,8,8]{2,1,5,4,3,0:T(8,128)(2,1)} copy(bf16[16,7,64,8,8,8]{2,5,4,3,0,1:T(8,128)(2,1)} %bitcast.418) | data formatting | bytes 14680064 | tf_op jit(solution)/shard_map/vmap()/transpose | solution.py:39
  118.9 22.2 %reshape.836 = bf16[16,448,512]{1,2,0:T(8,128)(2,1)} reshape(bf16[16,7,64,8,8,8]{2,1,5,4,3,0:T(8,128)(2,1)} %copy.344) | data formatting | bytes 14680064 | tf_op jit(solution)/shard_map/vmap()/reshape | solution.py:39
  141.1 6.5 %fusion.21 = (f32[16,16,512]{2,1,0:T(8,128)S(1)}, f32[16,16,512]{2,1,0:T(8,128)}) fusion(f32[16]{0:T(128)S(1)} %copy-done.27, bf16[16,448,512]{1,2,0:T(8,128)(2,1)} %reshape.836, bf16[16,448,1]{1,0,2:T(8,128)(2,1)S(1)} %reshape.951), kind=kOutput, calls=%fused_computation.62 | convolution fusion | flops 118358016 | bytes 8403008 | tf_op jit(solution)/shard_map/ln,bnp->blp/dot_general | solution.py:183
  147.6 3.7 copy.347
  160.1 12.0 %all_gather.7 = bf16[2,64,512]{2,1,0:T(8,128)(2,1)S(1)} all-gather(bf16[2,16,512]{2,1,0:T(8,128)(2,1)S(1)} %broadcast_select_fusion.4), channel_id=1, replica_groups=mesh['blocks'=64,'chan'=4] {'chan'}, dimensions={1}, use_global_device_ids=true | all-gather | bytes 163840 | tf_op jit(solution)/shard_map/all_gather | solution.py:202
  174.7 3.7 collective-permute-start.3
  181.9 4.3 copy.364
  195.2 5.9 %collective-permute-start.5 = (bf16[16,64]{1,0:T(8,128)(2,1)}, bf16[16,64]{1,0:T(8,128)(2,1)}, u32[]{:S(2)}, u32[]{:S(2)}) collective-permute-start(bf16[16,64]{1,0:T(8,128)(2,1)} %bitcast.86), channel_id=1, source_target_pairs={{0,4},{4,8},{8,12},{12,16},{16,20},{20,24},{24,28},{28,32},{32,36}... | collective-permute-start | bytes 6152 | tf_op jit(solution)/shard_map/ppermute | solution.py:13
  210.5 4.3 copy.383
  219.5 14.8 %copy.416 = bf16[448,16,512]{2,1,0:T(8,128)(2,1)} copy(bf16[448,16,512]{0,2,1:T(8,128)(2,1)} %bitcast.416) | data formatting | bytes 14680064 | tf_op jit(solution)/shard_map/blp,bnp->ln/dot_general | solution.py:272
  234.8 12.7 %reduce-scatter.3.cloned.1.call-done = bf16[2,16,512]{2,1,0:T(8,128)(2,1)} async-done(((bf16[2,64,512]{2,1,0:T(8,128)(2,1)}), bf16[2,16,512]{2,1,0:T(8,128)(2,1)}) %reduce-scatter.3.cloned.1.call-update) | async-done | bytes 32784 | tf_op jit(solution)/shard_map/reduce_scatter | solution.py:241
  251.3 3.5 collective-permute-done.7
  263.7 2.9 fusion.69
  269.6 3.0 fusion.67
  272.6 7.7 %fusion.18 = f32[7,16,64]{2,1,0:T(8,128)S(1)} fusion(bf16[7,64,16,512]{3,2,1,0:T(8,128)(2,1)S(1)} %bitcast.441, bf16[16,16,512]{2,1,0:T(8,128)(2,1)S(1)} %get-tuple-element.11), kind=kOutput, calls=%fused_computation.49 | convolution fusion | flops 117440512 | bytes 7630848 | tf_op jit(solution)/shard_map/blp,bnp->ln/dot_general | solution.py:272
  286.2 3.6 collective-permute-start.9
  313.4 33.5 %copy.413 = bf16[16,7,16,8,8,8]{2,1,5,4,3,0:T(8,128)(2,1)} copy(bf16[16,7,16,8,8,8]{2,5,4,3,0,1:T(8,128)(2,1)} %bitcast.417) | data formatting | bytes 3670016 | tf_op jit(solution)/shard_map/vmap()/transpose | solution.py:39
  346.9 17.2 %reshape.852 = bf16[16,112,512]{1,2,0:T(8,128)(2,1)S(1)} reshape(bf16[16,7,16,8,8,8]{2,1,5,4,3,0:T(8,128)(2,1)} %copy.413) | data formatting | bytes 3670016 | tf_op jit(solution)/shard_map/vmap()/reshape | solution.py:39
  366.7 170.5 %all-reduce.10.cloned.1.call-done = f32[4,14368]{1,0:T(4,128)} async-done(((f32[4,14368]{1,0:T(4,128)}), f32[4,14368]{1,0:T(4,128)}) %all-reduce.10.cloned.1.call-update) | async-done | bytes 229904 | tf_op jit(solution)/shard_map/psum | solution.py:143
  541.1 22.1 %reduce-scatter.5.cloned.1.call-done = bf16[16,16,512]{2,1,0:T(8,128)(2,1)} async-done(((bf16[16,64,512]{2,1,0:T(8,128)(2,1)}), bf16[16,16,512]{2,1,0:T(8,128)(2,1)}) %reduce-scatter.5.cloned.1.call-update) | async-done | bytes 262160 | tf_op jit(solution)/shard_map/reduce_scatter | solution.py:286
  (308 shorter events, 139.2 us)
Async XLA Ops:
  7.2 32.8 %all-gather.2.cloned.1.call-start = ((), (), s32[]{:S(2)}) async-start(), calls=%async_computation.2 | async-start | bytes 1310720 | tf_op jit(solution)/shard_map/all_gather | solution.py:175
  9.0 238.5 %reduce-scatter.3.cloned.1.call-start = ((), (), s32[]{:S(2)}) async-start(), calls=%async_computation.3 | async-start | bytes 163840 | tf_op jit(solution)/shard_map/reduce_scatter | solution.py:241
  25.6 153.9 %copy-start.26 = (pred[2]{0:T(512)(128)(4,1)}, pred[2]{0:T(512)(128)(4,1)S(1)}, u32[]{:S(2)}) copy-start(pred[2]{0:T(512)(128)(4,1)S(1)} %get-tuple-element.81) | copy-start | bytes 10
  25.6 154.8 %copy-start.25 = (pred[2]{0:T(512)(128)(4,1)}, pred[2]{0:T(512)(128)(4,1)S(1)}, u32[]{:S(2)}) copy-start(pred[2]{0:T(512)(128)(4,1)S(1)} %get-tuple-element.82) | copy-start | bytes 10
  25.6 153.3 %copy-start.24 = (s32[1024]{0:T(1024)}, s32[1024]{0:T(1024)S(1)}, u32[]{:S(2)}) copy-start(s32[1024]{0:T(1024)S(1)} %pad_clamp_fusion.2) | copy-start | bytes 12292
  25.6 154.2 %copy-start.23 = (s32[1024]{0:T(1024)}, s32[1024]{0:T(1024)S(1)}, u32[]{:S(2)}) copy-start(s32[1024]{0:T(1024)S(1)} %pad_clamp_fusion.3) | copy-start | bytes 12292
  53.0 7.2 %collective-permute-start = (bf16[4,3,64,64]{2,3,1,0:T(8,128)(2,1)S(1)}, bf16[4,3,64,64]{2,3,1,0:T(8,128)(2,1)S(1)}, u32[]{:S(2)}, u32[]{:S(2)}) collective-permute-start(bf16[4,3,64,64]{2,3,1,0:T(8,128)(2,1)S(1)} %constant_dynamic-slice_fusion.3), channel_id=1, source_target_pairs={{0,4},{4,8},{8,12},{12,16},{16,20},{20,24},{24,28},{28,32},{32,36}... | collective-permute-start | bytes 294920 | tf_op jit(solution)/shard_map/ppermute | solution.py:13
  54.9 8.7 %collective-permute-start.1 = (bf16[4,3,64,64]{2,3,1,0:T(8,128)(2,1)S(1)}, bf16[4,3,64,64]{2,3,1,0:T(8,128)(2,1)S(1)}, u32[]{:S(2)}, u32[]{:S(2)}) collective-permute-start(bf16[4,3,64,64]{2,3,1,0:T(8,128)(2,1)S(1)} %slice.370), channel_id=1, source_target_pairs={{4,0},{8,4},{12,8},{16,12},{20,16},{24,20},{28,24},{32,28},{36,32}... | collective-permute-start | bytes 294920 | tf_op jit(solution)/shard_map/ppermute | solution.py:13
  118.9 22.2 %copy-start.27 = (f32[16]{0:T(128)S(1)}, f32[16]{0:T(128)}, u32[]{:S(2)}) copy-start(f32[16]{0:T(128)} %param.13) | copy-start | bytes 196
  154.3 4.6 collective-permute-start.2
  156.3 31.0 %copy-start.28 = (pred[2]{0:T(512)(128)(4,1)}, pred[2]{0:T(512)(128)(4,1)S(1)}, u32[]{:S(2)}) copy-start(pred[2]{0:T(512)(128)(4,1)S(1)} %iota_compare_fusion.1) | copy-start | bytes 10
  172.8 6.1 %collective-permute-start.4 = (bf16[64,64]{0,1:T(8,128)(2,1)S(1)}, bf16[64,64]{0,1:T(8,128)(2,1)S(1)}, u32[]{:S(2)}, u32[]{:S(2)}) collective-permute-start(bf16[64,64]{0,1:T(8,128)(2,1)S(1)} %slice_bitcast_fusion.31), channel_id=1, source_target_pairs={{4,0},{8,4},{12,8},{16,12},{20,16},{24,20},{28,24},{32,28},{36,32}... | collective-permute-start | bytes 24584 | tf_op jit(solution)/shard_map/ppermute | solution.py:13
  174.7 5.1 collective-permute-start.3
  192.6 11.0 %collective-permute-start.6 = (bf16[16,64]{0,1:T(8,128)(2,1)}, bf16[16,64]{0,1:T(8,128)(2,1)}, u32[]{:S(2)}, u32[]{:S(2)}) collective-permute-start(bf16[16,64]{0,1:T(8,128)(2,1)} %slice_bitcast_fusion.30), channel_id=1, source_target_pairs={{4,0},{8,4},{12,8},{16,12},{20,16},{24,20},{28,24},{32,28},{36,32}... | collective-permute-start | bytes 6152 | tf_op jit(solution)/shard_map/ppermute | solution.py:13
  195.2 8.2 %copy-start.19 = (bf16[2,16,8,7,8]{1,4,3,2,0:T(8,128)(2,1)S(1)}, bf16[2,16,8,7,8]{1,4,3,2,0:T(8,128)(2,1)}, u32[]{:S(2)}) copy-start(bf16[2,16,8,7,8]{1,4,3,2,0:T(8,128)(2,1)} %get-tuple-element.48) | copy-start | bytes 86020
  195.2 10.8 %collective-permute-start.5 = (bf16[16,64]{1,0:T(8,128)(2,1)}, bf16[16,64]{1,0:T(8,128)(2,1)}, u32[]{:S(2)}, u32[]{:S(2)}) collective-permute-start(bf16[16,64]{1,0:T(8,128)(2,1)} %bitcast.86), channel_id=1, source_target_pairs={{0,4},{4,8},{8,12},{12,16},{16,20},{20,24},{24,28},{28,32},{32,36}... | collective-permute-start | bytes 6152 | tf_op jit(solution)/shard_map/ppermute | solution.py:13
  217.1 320.1 %all-reduce.10.cloned.1.call-start = ((), (), s32[]{:S(2)}) async-start(), calls=%async_computation.5 | async-start | bytes 462848 | tf_op jit(solution)/shard_map/psum | solution.py:143
  219.5 28.0 %copy-start.29 = (pred[2]{0:T(512)(128)(4,1)S(1)}, pred[2]{0:T(512)(128)(4,1)}, u32[]{:S(2)}) copy-start(pred[2]{0:T(512)(128)(4,1)} %copy-done.28) | copy-start | bytes 10
  248.7 6.1 %collective-permute-start.7 = (bf16[7,16,64]{1,2,0:T(8,128)(2,1)S(1)}, bf16[7,16,64]{1,2,0:T(8,128)(2,1)S(1)}, u32[]{:S(2)}, u32[]{:S(2)}) collective-permute-start(bf16[7,16,64]{1,2,0:T(8,128)(2,1)S(1)} %constant_dynamic-slice_fusion.1), channel_id=1, source_target_pairs={{0,4},{4,8},{8,12},{12,16},{16,20},{20,24},{24,28},{28,32},{32,36}... | collective-permute-start | bytes 43016 | tf_op jit(solution)/shard_map/ppermute | solution.py:13
  263.7 8.9 %slice-start = ((s8[7340032]{0:T(1024)(128)(4,1)}), s8[4194304]{0:T(1024)(128)(4,1)S(1)}, s32[]{:S(2)}) async-start(s8[7340032]{0:T(1024)(128)(4,1)} %bitcast.439), calls=%async_computation.6 | async-start | bytes 8388608
  282.6 280.6 %reduce-scatter.5.cloned.1.call-start = ((), (), s32[]{:S(2)}) async-start(), calls=%async_computation.4 | async-start | bytes 1310720 | tf_op jit(solution)/shard_map/reduce_scatter | solution.py:286
  284.2 9.0 %collective-permute-start.8 = (bf16[4,3,16,64]{2,3,1,0:T(8,128)(2,1)S(1)}, bf16[4,3,16,64]{2,3,1,0:T(8,128)(2,1)}, u32[]{:S(2)}, u32[]{:S(2)}) collective-permute-start(bf16[4,3,16,64]{2,3,1,0:T(8,128)(2,1)S(1)} %constant_dynamic-slice_fusion), channel_id=1, source_target_pairs={{0,4},{4,8},{8,12},{12,16},{16,20},{20,24},{24,28},{28,32},{32,36}... | collective-permute-start | bytes 73736 | tf_op jit(solution)/shard_map/ppermute | solution.py:13
  286.2 9.1 %collective-permute-start.9 = (bf16[4,3,16,64]{2,3,1,0:T(8,128)(2,1)S(1)}, bf16[4,3,16,64]{2,3,1,0:T(8,128)(2,1)S(1)}, u32[]{:S(2)}, u32[]{:S(2)}) collective-permute-start(bf16[4,3,16,64]{2,3,1,0:T(8,128)(2,1)S(1)} %slice.420), channel_id=1, source_target_pairs={{4,0},{8,4},{12,8},{16,12},{20,16},{24,20},{28,24},{32,28},{36,32}... | collective-permute-start | bytes 73736 | tf_op jit(solution)/shard_map/ppermute | solution.py:13
  346.9 17.2 %copy-start.20 = (bf16[7,16,64]{2,1,0:T(8,128)(2,1)S(1)}, bf16[7,16,64]{2,1,0:T(8,128)(2,1)}, u32[]{:S(2)}) copy-start(bf16[7,16,64]{2,1,0:T(8,128)(2,1)} %gather_fusion.11) | copy-start | bytes 43012
  (25 other events, 67.1 us)
Sparse Core Ops, SparseCore 0:
  10.4 29.5 all-gather.1
  217.2 30.2 reduce-scatter.2
  282.7 254.4 all-reduce.9
  539.6 23.5 reduce-scatter.4
where the time goes:
time: 580 us; the launch traced here: 572 us
  waiting for transfers between devices  224 us (39%)
  local copies, waits for them, and re-layouts  217 us (37%)
  other arithmetic  48.9 us (8%)
  starting transfers between devices  28.5 us (5%)
  between operations  21.9 us (4%)
  matrix products  19.2 us (3%)
  blocking collectives  12 us (2%)
    psum x1, waiting for transfers between devices, sum_over_blocks(): summed = lax.psum(slots, ('blocks', 'chan'))  170 us
    transpose x4, local copies, waits for them, and re-layouts, block_views(): return stacked.reshape(7 * channels, edge_cells ** 3)  75.6 us
    reshape x4, local copies, waits for them, and re-layouts, block_views(): return stacked.reshape(7 * channels, edge_cells ** 3)  41.7 us
    ppermute x10, starting transfers between devices, from_behind(): return lax.ppermute(block, axis, route)  28.4 us
    unnamed x13, other arithmetic  23.8 us
    reduce_scatter x1, waiting for transfers between devices, local(): lax.psum_scatter(fine_partial.astype(jnp.bfloat16), 'chan', scatter_dimen...  22.1 us
    dot_general x1, local copies, waits for them, and re-layouts, local(): jnp.einsum('blp,bnp->ln', fine_delta, fine_views, preferred_element_type=...  14.8 us
    unnamed x103, local copies, waits for them, and re-layouts  13.7 us
  transfers between devices with their start and end apart: 14, of which 7 were waited for; matrix products, arithmetic and copies ran while one was open for 21% of the time, Pallas kernels for 0%

commit v1 on v0

--- a/solution.py
+++ b/solution.py
@@ -172,7 +172,15 @@
     coarse_ids = coarse_first + jnp.arange(coarse_slots, dtype=jnp.int32)
     live_mask = (jnp.arange(slot_count) < live_count)[:, None, None]
     coarse_live = (jnp.arange(coarse_slots) < coarse_count)[:, None, None]
-    full_input = lax.all_gather(fine_input, "chan", axis=1, tiled=True)
+    full_input = jnp.concatenate(
+        lax.all_to_all(
+            jnp.stack([fine_input for _ in range(lax.axis_size("chan"))]),
+            axis_name="chan",
+            split_axis=0,
+            concat_axis=0,
+        ),
+        axis=1,
+    )
     fine_cubes = full_input.reshape(slot_count, channels, EDGE, EDGE, EDGE)
     input_halos = fine_halo(
         jax.vmap(block_layers)(fine_cubes), block_ids, first_block, live_count, total_blocks

time: 580 us -> 601 us (1.036)
  local copies, waits for them, and re-layouts: 217 us -> 242 us
  waiting for transfers between devices: 224 us -> 214 us
  starting transfers between devices: 28.5 us -> 34.9 us
    another operation x1 -> x4, local copies, waits for them, and re-layouts: 0.74 us -> 22.3 us  [the longest x1 10.5 us: block_views(): jnp.stack([block_cube, minus_x, plus_x, minus_y, plus_y, minus_z, plus_z])]
    all_gather x1 -> x0, waiting for transfers between devices: 13.6 us -> none  [local(): full_input = lax.all_gather(fine_input, 'chan', axis=1, tiled=True)]
    reshape x0 -> x1, local copies, waits for them, and re-layouts: none -> 8.94 us  [local(): jnp.concatenate(lax.all_to_all(jnp.stack([fine_input for _ in range(lax.a...]
    unnamed x103 -> x114, local copies, waits for them, and re-layouts: 13.7 us -> 11.9 us
  transfers between devices with their start and end apart: 14 -> 14, of which waited for: 7 -> 8; matrix products, arithmetic and copies ran while one was open for 21% -> 20% of each run, Pallas kernels for 0% -> 0%
where the time goes in v1:
time: 601 us; the launch traced here: 591 us
  local copies, waits for them, and re-layouts  242 us (40%)
  waiting for transfers between devices  214 us (36%)
  other arithmetic  46.8 us (8%)
  starting transfers between devices  34.9 us (6%)
  between operations  22.2 us (4%)
  matrix products  19.2 us (3%)
  blocking collectives  12 us (2%)
    psum x1, waiting for transfers between devices, sum_over_blocks(): summed = lax.psum(slots, ('blocks', 'chan'))  170 us
    transpose x4, local copies, waits for them, and re-layouts, block_views(): return stacked.reshape(7 * channels, edge_cells ** 3)  75.6 us
    reshape x4, local copies, waits for them, and re-layouts, block_views(): return stacked.reshape(7 * channels, edge_cells ** 3)  41.8 us
    ppermute x10, starting transfers between devices, from_behind(): return lax.ppermute(block, axis, route)  30.4 us
    unnamed x13, other arithmetic  23.8 us
    reduce_scatter x1, waiting for transfers between devices, local(): lax.psum_scatter(fine_partial.astype(jnp.bfloat16), 'chan', scatter_dimen...  22.3 us
    dot_general x1, local copies, waits for them, and re-layouts, local(): jnp.einsum('blp,bnp->ln', fine_delta, fine_views, preferred_element_type=...  14.8 us
    reduce_scatter x1, waiting for transfers between devices, local(): lax.psum_scatter(partial_sums.astype(jnp.bfloat16), 'chan', scatter_dimen...  14 us
  transfers between devices with their start and end apart: 14, of which 8 were waited for; matrix products, arithmetic and copies ran while one was open for 20% of the time, Pallas kernels for 0%

profile of v1, /device:TPU:6, one launch (start us, length us, event | category | flops | bytes accessed | tf_op | source)
XLA Modules:
  0.0 591.3 jit_solution(3378192622714761717)
XLA Ops:
  9.4 4.5 all-to-all-start
  28.9 8.9 %copy.322 = bf16[16,4,16,512]{2,1,3,0:T(4,128)(2,1)} copy(bf16[16,4,16,512]{3,2,0,1:T(8,128)(2,1)S(1)} %bitcast.438) | data formatting | bytes 2097152 | tf_op jit(solution)/shard_map/reshape | solution.py:175
  37.9 9.5 %reshape_reshape.9 = bf16[16,64,8,8,8]{1,4,3,2,0:T(8,128)(2,1)S(1)} reshape(bf16[16,4,16,512]{2,1,3,0:T(4,128)(2,1)} %copy.322) | data formatting | bytes 2097152 | tf_op jit(solution)/shard_map/reshape;reshape | solution.py:184
  51.5 10.5 %stack_reshape_reshape.3 = bf16[1,16,64,8,8,8]{2,5,4,3,1,0:T(8,128)(2,1)} reshape(bf16[16,4,16,512]{2,1,3,0:T(4,128)(2,1)} %copy.322) | data formatting | bytes 2097152 | tf_op jit(solution)/shard_map/vmap()/stack;reshape;reshape | solution.py:38
  70.7 3.6 collective-permute-start.1
  101.2 33.5 %copy.341 = bf16[16,7,64,8,8,8]{2,1,5,4,3,0:T(8,128)(2,1)} copy(bf16[16,7,64,8,8,8]{2,5,4,3,0,1:T(8,128)(2,1)} %bitcast.412) | data formatting | bytes 14680064 | tf_op jit(solution)/shard_map/vmap()/transpose | solution.py:39
  134.7 22.2 %reshape.838 = bf16[16,448,512]{1,2,0:T(8,128)(2,1)} reshape(bf16[16,7,64,8,8,8]{2,1,5,4,3,0:T(8,128)(2,1)} %copy.341) | data formatting | bytes 14680064 | tf_op jit(solution)/shard_map/vmap()/reshape | solution.py:39
  156.9 6.5 %fusion.21 = (f32[16,16,512]{2,1,0:T(8,128)S(1)}, f32[16,16,512]{2,1,0:T(8,128)}) fusion(f32[16]{0:T(128)S(1)} %copy-done.29, bf16[16,448,512]{1,2,0:T(8,128)(2,1)} %reshape.838, bf16[16,448,1]{1,0,2:T(8,128)(2,1)S(1)} %reshape.953), kind=kOutput, calls=%fused_computation.62 | convolution fusion | flops 118358016 | bytes 8403008 | tf_op jit(solution)/shard_map/ln,bnp->blp/dot_general | solution.py:191
  163.4 3.7 copy.344
  170.1 3.8 collective-permute-start.2
  178.0 12.0 %all_gather.3 = bf16[2,64,512]{2,1,0:T(8,128)(2,1)S(1)} all-gather(bf16[2,16,512]{2,1,0:T(8,128)(2,1)S(1)} %broadcast_select_fusion.4), channel_id=1, replica_groups=mesh['blocks'=64,'chan'=4] {'chan'}, dimensions={1}, use_global_device_ids=true | all-gather | bytes 163840 | tf_op jit(solution)/shard_map/all_gather | solution.py:210
  192.7 3.7 collective-permute-start.3
  199.8 4.3 copy.361
  213.1 5.9 collective-permute-start.5
  228.4 4.3 copy.380
  237.5 14.8 %copy.413 = bf16[448,16,512]{2,1,0:T(8,128)(2,1)} copy(bf16[448,16,512]{0,2,1:T(8,128)(2,1)} %bitcast.410) | data formatting | bytes 14680064 | tf_op jit(solution)/shard_map/blp,bnp->ln/dot_general | solution.py:280
  252.8 14.0 %reduce-scatter.3.cloned.1.call-done = bf16[2,16,512]{2,1,0:T(8,128)(2,1)} async-done(((bf16[2,64,512]{2,1,0:T(8,128)(2,1)}), bf16[2,16,512]{2,1,0:T(8,128)(2,1)}) %reduce-scatter.3.cloned.1.call-update) | async-done | bytes 32784 | tf_op jit(solution)/shard_map/reduce_scatter | solution.py:249
  270.5 3.5 collective-permute-done.7
  291.9 7.7 %fusion.18 = f32[7,16,64]{2,1,0:T(8,128)S(1)} fusion(bf16[7,64,16,512]{3,2,1,0:T(8,128)(2,1)S(1)} %bitcast.435, bf16[16,16,512]{2,1,0:T(8,128)(2,1)S(1)} %get-tuple-element.11), kind=kOutput, calls=%fused_computation.49 | convolution fusion | flops 117440512 | bytes 7630848 | tf_op jit(solution)/shard_map/blp,bnp->ln/dot_general | solution.py:280
  305.4 3.6 collective-permute-start.9
  332.7 33.5 %copy.410 = bf16[16,7,16,8,8,8]{2,1,5,4,3,0:T(8,128)(2,1)} copy(bf16[16,7,16,8,8,8]{2,5,4,3,0,1:T(8,128)(2,1)} %bitcast.411) | data formatting | bytes 3670016 | tf_op jit(solution)/shard_map/vmap()/transpose | solution.py:39
  366.2 17.2 %reshape.854 = bf16[16,112,512]{1,2,0:T(8,128)(2,1)S(1)} reshape(bf16[16,7,16,8,8,8]{2,1,5,4,3,0:T(8,128)(2,1)} %copy.410) | data formatting | bytes 3670016 | tf_op jit(solution)/shard_map/vmap()/reshape | solution.py:39
  386.0 170.4 %all-reduce.10.cloned.1.call-done = f32[4,14368]{1,0:T(4,128)} async-done(((f32[4,14368]{1,0:T(4,128)}), f32[4,14368]{1,0:T(4,128)}) %all-reduce.10.cloned.1.call-update) | async-done | bytes 229904 | tf_op jit(solution)/shard_map/psum | solution.py:143
  560.2 22.3 %reduce-scatter.5.cloned.1.call-done = bf16[16,16,512]{2,1,0:T(8,128)(2,1)} async-done(((bf16[16,64,512]{2,1,0:T(8,128)(2,1)}), bf16[16,16,512]{2,1,0:T(8,128)(2,1)}) %reduce-scatter.5.cloned.1.call-update) | async-done | bytes 262160 | tf_op jit(solution)/shard_map/reduce_scatter | solution.py:294
  (321 shorter events, 145.1 us)
Async XLA Ops:
  7.2 17.4 %copy-start.35 = (s32[3]{0:T(128)S(1)}, s32[3]{0:T(128)}, u32[]{:S(2)}) copy-start(s32[3]{0:T(128)} %constant.184.clone) | copy-start | bytes 40
  7.2 20.1 %copy-start.34 = (s32[7]{0:T(128)S(1)}, s32[7]{0:T(128)}, u32[]{:S(2)}) copy-start(s32[7]{0:T(128)} %constant.260) | copy-start | bytes 88
  7.2 19.8 %copy-start.23 = (bf16[7,16,64]{2,1,0:T(8,128)(2,1)S(1)}, bf16[7,16,64]{2,1,0:T(8,128)(2,1)}, u32[]{:S(2)}) copy-start(bf16[7,16,64]{2,1,0:T(8,128)(2,1)} %param.12) | copy-start | bytes 43012
  9.4 19.6 %all-to-all-start = ((bf16[4,16,16,512]{3,2,1,0:T(8,128)(2,1)}), bf16[4,16,16,512]{3,2,1,0:T(8,128)(2,1)S(1)}, u32[]{:S(2)}, u32[]{:S(2)}) async-start(bf16[4,16,16,512]{3,2,1,0:T(8,128)(2,1)} %stack.141), calls=%async_computation | async-start | bytes 2097152 | tf_op jit(solution)/shard_map/all_to_all | solution.py:176
  13.8 252.9 %reduce-scatter.3.cloned.1.call-start = ((), (), s32[]{:S(2)}) async-start(), calls=%async_computation.3 | async-start | bytes 163840 | tf_op jit(solution)/shard_map/reduce_scatter | solution.py:249
  27.2 170.2 %copy-start.28 = (pred[2]{0:T(512)(128)(4,1)}, pred[2]{0:T(512)(128)(4,1)S(1)}, u32[]{:S(2)}) copy-start(pred[2]{0:T(512)(128)(4,1)S(1)} %get-tuple-element.81) | copy-start | bytes 10
  27.3 171.1 %copy-start.27 = (pred[2]{0:T(512)(128)(4,1)}, pred[2]{0:T(512)(128)(4,1)S(1)}, u32[]{:S(2)}) copy-start(pred[2]{0:T(512)(128)(4,1)S(1)} %get-tuple-element.82) | copy-start | bytes 10
  27.3 169.6 %copy-start.26 = (s32[1024]{0:T(1024)}, s32[1024]{0:T(1024)S(1)}, u32[]{:S(2)}) copy-start(s32[1024]{0:T(1024)S(1)} %pad_clamp_fusion.2) | copy-start | bytes 12292
  27.3 170.4 %copy-start.25 = (s32[1024]{0:T(1024)}, s32[1024]{0:T(1024)S(1)}, u32[]{:S(2)}) copy-start(s32[1024]{0:T(1024)S(1)} %pad_clamp_fusion.3) | copy-start | bytes 12292
  68.6 7.2 %collective-permute-start = (bf16[4,3,64,64]{2,3,1,0:T(8,128)(2,1)S(1)}, bf16[4,3,64,64]{2,3,1,0:T(8,128)(2,1)S(1)}, u32[]{:S(2)}, u32[]{:S(2)}) collective-permute-start(bf16[4,3,64,64]{2,3,1,0:T(8,128)(2,1)S(1)} %constant_dynamic-slice_fusion.3), channel_id=1, source_target_pairs={{0,4},{4,8},{8,12},{12,16},{16,20},{20,24},{24,28},{28,32},{32,36}... | collective-permute-start | bytes 294920 | tf_op jit(solution)/shard_map/ppermute | solution.py:13
  70.7 6.8 %collective-permute-start.1 = (bf16[4,3,64,64]{2,3,1,0:T(8,128)(2,1)S(1)}, bf16[4,3,64,64]{2,3,1,0:T(8,128)(2,1)S(1)}, u32[]{:S(2)}, u32[]{:S(2)}) collective-permute-start(bf16[4,3,64,64]{2,3,1,0:T(8,128)(2,1)S(1)} %slice.370), channel_id=1, source_target_pairs={{4,0},{8,4},{12,8},{16,12},{20,16},{24,20},{28,24},{32,28},{36,32}... | collective-permute-start | bytes 294920 | tf_op jit(solution)/shard_map/ppermute | solution.py:13
  134.7 22.3 %copy-start.29 = (f32[16]{0:T(128)S(1)}, f32[16]{0:T(128)}, u32[]{:S(2)}) copy-start(f32[16]{0:T(128)} %param.13) | copy-start | bytes 196
  170.1 6.8 %collective-permute-start.2 = (bf16[7,16,64]{2,1,0:T(8,128)(2,1)S(1)}, bf16[7,16,64]{2,1,0:T(8,128)(2,1)S(1)}, u32[]{:S(2)}, u32[]{:S(2)}) collective-permute-start(bf16[7,16,64]{2,1,0:T(8,128)(2,1)S(1)} %copy.346), channel_id=1, source_target_pairs={{4,0},{8,4},{12,8},{16,12},{20,16},{24,20},{28,24},{32,28},{36,32}... | collective-permute-start | bytes 43016 | tf_op jit(solution)/shard_map/ppermute | solution.py:13
  173.9 31.3 %copy-start.30 = (pred[2]{0:T(512)(128)(4,1)}, pred[2]{0:T(512)(128)(4,1)S(1)}, u32[]{:S(2)}) copy-start(pred[2]{0:T(512)(128)(4,1)S(1)} %iota_compare_fusion.1) | copy-start | bytes 10
  190.7 6.1 %collective-permute-start.4 = (bf16[64,64]{0,1:T(8,128)(2,1)S(1)}, bf16[64,64]{0,1:T(8,128)(2,1)S(1)}, u32[]{:S(2)}, u32[]{:S(2)}) collective-permute-start(bf16[64,64]{0,1:T(8,128)(2,1)S(1)} %slice_bitcast_fusion.31), channel_id=1, source_target_pairs={{4,0},{8,4},{12,8},{16,12},{20,16},{24,20},{28,24},{32,28},{36,32}... | collective-permute-start | bytes 24584 | tf_op jit(solution)/shard_map/ppermute | solution.py:13
  192.7 5.1 collective-permute-start.3
  210.5 11.0 %collective-permute-start.6 = (bf16[16,64]{0,1:T(8,128)(2,1)}, bf16[16,64]{0,1:T(8,128)(2,1)}, u32[]{:S(2)}, u32[]{:S(2)}) collective-permute-start(bf16[16,64]{0,1:T(8,128)(2,1)} %slice_bitcast_fusion.30), channel_id=1, source_target_pairs={{4,0},{8,4},{12,8},{16,12},{20,16},{24,20},{28,24},{32,28},{36,32}... | collective-permute-start | bytes 6152 | tf_op jit(solution)/shard_map/ppermute | solution.py:13
  213.1 10.8 %collective-permute-start.5 = (bf16[16,64]{1,0:T(8,128)(2,1)}, bf16[16,64]{1,0:T(8,128)(2,1)}, u32[]{:S(2)}, u32[]{:S(2)}) collective-permute-start(bf16[16,64]{1,0:T(8,128)(2,1)} %bitcast.85), channel_id=1, source_target_pairs={{0,4},{4,8},{8,12},{12,16},{16,20},{20,24},{24,28},{28,32},{32,36}... | collective-permute-start | bytes 6152 | tf_op jit(solution)/shard_map/ppermute | solution.py:13
  234.9 321.4 %all-reduce.10.cloned.1.call-start = ((), (), s32[]{:S(2)}) async-start(), calls=%async_computation.5 | async-start | bytes 462848 | tf_op jit(solution)/shard_map/psum | solution.py:143
  237.5 29.2 %copy-start.31 = (pred[2]{0:T(512)(128)(4,1)S(1)}, pred[2]{0:T(512)(128)(4,1)}, u32[]{:S(2)}) copy-start(pred[2]{0:T(512)(128)(4,1)} %copy-done.30) | copy-start | bytes 10
  267.9 6.1 %collective-permute-start.7 = (bf16[7,16,64]{1,2,0:T(8,128)(2,1)S(1)}, bf16[7,16,64]{1,2,0:T(8,128)(2,1)S(1)}, u32[]{:S(2)}, u32[]{:S(2)}) collective-permute-start(bf16[7,16,64]{1,2,0:T(8,128)(2,1)S(1)} %constant_dynamic-slice_fusion.1), channel_id=1, source_target_pairs={{0,4},{4,8},{8,12},{12,16},{16,20},{20,24},{24,28},{28,32},{32,36}... | collective-permute-start | bytes 43016 | tf_op jit(solution)/shard_map/ppermute | solution.py:13
  301.8 280.7 %reduce-scatter.5.cloned.1.call-start = ((), (), s32[]{:S(2)}) async-start(), calls=%async_computation.4 | async-start | bytes 1310720 | tf_op jit(solution)/shard_map/reduce_scatter | solution.py:294
  303.5 8.9 %collective-permute-start.8 = (bf16[4,3,16,64]{2,3,1,0:T(8,128)(2,1)S(1)}, bf16[4,3,16,64]{2,3,1,0:T(8,128)(2,1)}, u32[]{:S(2)}, u32[]{:S(2)}) collective-permute-start(bf16[4,3,16,64]{2,3,1,0:T(8,128)(2,1)S(1)} %constant_dynamic-slice_fusion), channel_id=1, source_target_pairs={{0,4},{4,8},{8,12},{12,16},{16,20},{20,24},{24,28},{28,32},{32,36}... | collective-permute-start | bytes 73736 | tf_op jit(solution)/shard_map/ppermute | solution.py:13
  305.4 9.1 %collective-permute-start.9 = (bf16[4,3,16,64]{2,3,1,0:T(8,128)(2,1)S(1)}, bf16[4,3,16,64]{2,3,1,0:T(8,128)(2,1)S(1)}, u32[]{:S(2)}, u32[]{:S(2)}) collective-permute-start(bf16[4,3,16,64]{2,3,1,0:T(8,128)(2,1)S(1)} %slice.420), channel_id=1, source_target_pairs={{4,0},{8,4},{12,8},{16,12},{20,16},{24,20},{28,24},{32,28},{36,32}... | collective-permute-start | bytes 73736 | tf_op jit(solution)/shard_map/ppermute | solution.py:13
  (31 other events, 133.2 us)
Sparse Core Ops, SparseCore 0:
  235.1 31.6 reduce-scatter.2
  301.9 254.3 all-reduce.9
  558.9 23.5 reduce-scatter.4
